TPU v7x, 256 devices: a whole 4x4x8 slice. The times are simulated.
256 devices in a mesh: gx: 8 (over z), gy: 32 (over y, x, core).
Axes of the slice: x: 4, y: 4, z: 8, core: 2. Of those that a mesh axis runs over, the one named last changes fastest.
Arguments:
- lengths: int32 [17], replicated, may hold values from 16 to 16384, as said below
- page_table: int32 [1169], replicated, may hold values from 0 to 1287, as said below
- projected: bfloat16 [18432, 9216], P('gx', 'gy'), may hold values from -8 to 8
- residual: bfloat16 [18432, 3072], P('gx', 'gy'), may hold values from -6 to 6
- out_weight: bfloat16 [3072, 3072], P('gx', 'gy'), may hold values from -0.109375 to 0.109375
Outputs:
- hidden: bfloat16 [18432, 3072], P('gx', 'gy')
- cache_pages: bfloat16 [1288, 32, 3072], P('gx', 'gy')
Inputs may be any that keep to these rules, and one draw needn't show every extreme that they name: `lengths`: one prompt of 16384 tokens at a place drawn from the seed and 16 short prompts of 16 to 240 tokens; they sum to 18432. `page_table`: entry g is the physical page of logical page g (the pages of each prompt in order, 16 tokens each, prompts in packing order). Distinct logical pages in use get distinct physical pages, and such a page lies in [d * 161, (d + 1) * 161) where d is the index of gx whose tokens hold the page's first token. Entries past the last logical page in use are arbitrary; the last two entries are never in use and hold 0 and 1287.
All inputs are finite; a program needn't handle non-finite values.
Results may differ from a plain program's by a relative error of at most 0.012.
The roundings to bfloat16 on the way count: a program that leaves them out, or rounds other values in their place, can miss the bound.
Values may be sent and summed in bfloat16 or wider, within the bound.
No kernel may reach another device: no remote copies, remote signals or barrier semaphores. Data moves between devices by JAX's collectives and lax.ppermute only.
A program may use at most 128 MiB of HBM per device.

v0:
```python
from functools import partial
import math
import jax
import jax.numpy as jnp
from jax import lax
from jax.sharding import PartitionSpec as P

HD = 96
PAGE = 16


def passed_along(block, axis, distance):
    devices = range(lax.axis_size(axis))
    route = [(i - distance, i) for i in devices if i - distance in devices]
    return lax.ppermute(block, axis, route)


def segment_of(ends_at, token_index):
    return jnp.sum((ends_at[None, :] <= token_index[:, None]).astype(jnp.int32), axis=1)


def rotate(values, position):
    half_size = HD // 2
    inverse = 10000.0 ** (-(jnp.arange(half_size, dtype=jnp.float32) * 2.0) / HD)
    angle = position.astype(jnp.float32)[:, None, None] * inverse[None, None, :]
    cosine = jnp.cos(angle)
    sine_part = jnp.sin(angle)
    widened = values.astype(jnp.float32)
    front_half = widened[..., :half_size]
    back_half = widened[..., half_size:]
    turned = jnp.concatenate(
        [front_half * cosine - back_half * sine_part, back_half * cosine + front_half * sine_part],
        axis=-1,
    )
    return turned.astype(jnp.bfloat16)


def tile_update(
    query_block,
    query_segment,
    query_index,
    key_block,
    value_block,
    key_segment,
    key_index,
    carry_state,
):
    running_max, running_sum, running_acc = carry_state
    scores = jnp.einsum(
        "qhd,khd->hqk", query_block, key_block, preferred_element_type=jnp.float32
    ) * (1.0 / math.sqrt(HD))
    visible = (query_segment[:, None] == key_segment[None, :]) & (
        query_index[:, None] >= key_index[None, :]
    )
    scores = jnp.where(visible[None], scores, -1e30)
    new_max = jnp.maximum(running_max, jnp.max(scores, axis=2))
    weights = jnp.where(visible[None], jnp.exp(scores - new_max[:, :, None]), 0.0)
    factor = jnp.exp(running_max - new_max)
    new_sum = running_sum * factor + jnp.sum(weights, axis=2)
    new_acc = running_acc * factor[:, :, None] + jnp.einsum(
        "hqk,khd->hqd",
        weights.astype(jnp.bfloat16),
        value_block,
        preferred_element_type=jnp.float32,
    )
    return (new_max, new_sum, new_acc)


def keep_state(carry_state):
    return carry_state


def per_device(lengths, page_table, projected, residual, out_weight):
    row_count = projected.shape[0]
    local_heads = projected.shape[1] // (3 * HD)
    group_size = lax.axis_size("gx")
    group_index = lax.axis_index("gx")
    first_row = group_index * row_count
    ends_at = jnp.cumsum(lengths)
    starts_at = ends_at - lengths
    own_index = first_row + jnp.arange(row_count, dtype=jnp.int32)
    own_segment = segment_of(ends_at, own_index)
    own_position = own_index - starts_at[own_segment]
    split_heads = projected.reshape(row_count, local_heads, 3, HD)
    rotated_queries = rotate(split_heads[:, :, 0], own_position)
    rotated_keys = rotate(split_heads[:, :, 1], own_position)
    key_value = jnp.concatenate([rotated_keys, split_heads[:, :, 2]], axis=-1)
    half_rows = row_count // 2
    query_segment = segment_of(ends_at, own_index)
    query_rows = half_rows // max(1, half_rows // 576)
    block_count = row_count // query_rows
    query_blocks = [
        rotated_queries[number * query_rows : (number + 1) * query_rows]
        for number in range(block_count)
    ]
    initial = tuple(
        (
            (
                jnp.full((local_heads, query_rows), -1e30, jnp.float32),
                jnp.zeros((local_heads, query_rows), jnp.float32),
                jnp.zeros((local_heads, query_rows, HD), jnp.float32),
            )
            for number in range(block_count)
        )
    )
    portion = lax.all_gather(key_value, "gx", axis=0, tiled=True)
    key_count = portion.shape[0]
    key_rows = key_count // max(1, key_count // 1152)
    steps_needed = key_count // key_rows
    key_index = jnp.arange(key_count, dtype=jnp.int32)
    key_segment = segment_of(ends_at, key_index)
    scanned_input = (
        portion.reshape(steps_needed, key_rows, local_heads, 2 * HD),
        key_index.reshape(steps_needed, key_rows),
        key_segment.reshape(steps_needed, key_rows),
    )

    def advance(block_states, scanned):
        key_block, block_index, block_segment = scanned
        updated = []
        for number in range(block_count):
            lower_row = number * query_rows
            upper_row = lower_row + query_rows
            live = (block_index[0] <= own_index[upper_row - 1]) & (
                block_segment[key_rows - 1] >= query_segment[lower_row]
            )
            working = partial(
                tile_update,
                query_blocks[number],
                query_segment[lower_row:upper_row],
                own_index[lower_row:upper_row],
                key_block[:, :, :HD],
                key_block[:, :, HD:],
                block_segment,
                block_index,
            )
            updated.append(lax.cond(live, working, keep_state, block_states[number]))
        return (tuple(updated), None)

    folded = lax.scan(advance, initial, scanned_input)[0]
    pieces = []
    for number in range(block_count):
        running_max, running_sum, running_acc = folded[number]
        normalized = (running_acc / running_sum[:, :, None]).astype(jnp.bfloat16)
        pieces.append(jnp.swapaxes(normalized, 0, 1).reshape(query_rows, local_heads * HD))
    attended = jnp.concatenate(pieces, axis=0)
    weight_columns = lax.all_gather(out_weight, "gx", axis=0, tiled=True)
    update = jnp.dot(
        lax.all_gather(attended, "gy", axis=1, tiled=True),
        weight_columns,
        preferred_element_type=jnp.float32,
    )
    hidden = (residual.astype(jnp.float32) + update).astype(jnp.bfloat16)
    tail_rows = passed_along(key_value[: PAGE - 1], "gx", -1)
    extended = jnp.concatenate([key_value, tail_rows], axis=0)
    extended_index = first_row + jnp.arange(row_count + PAGE - 1, dtype=jnp.int32)
    extended_segment = jnp.minimum(segment_of(ends_at, extended_index), lengths.shape[0] - 1)
    extended_position = extended_index - starts_at[extended_segment]
    page_count = (lengths + PAGE - 1) // PAGE
    page_base = jnp.cumsum(page_count) - page_count
    logical = page_base[extended_segment] + extended_position // PAGE
    page_first = extended_index - extended_position % PAGE
    pages_held = row_count // PAGE + lengths.shape[0]
    owned = (page_first // row_count == group_index) & (extended_index < group_size * row_count)
    target = jnp.where(owned, page_table[logical] - group_index * pages_held, pages_held)
    cache_pages = jnp.zeros((pages_held, local_heads, PAGE, 2 * HD), jnp.bfloat16)
    cache_pages = cache_pages.at[target, :, extended_position % PAGE].set(extended, mode="drop")
    return (hidden, cache_pages.reshape(pages_held, local_heads, PAGE * 2 * HD))


def solution(mesh):
    placed = (P(), P(), P("gx", "gy"), P("gx", "gy"), P("gx", "gy"))
    return jax.shard_map(
        per_device,
        mesh=mesh,
        in_specs=placed,
        out_specs=(P("gx", "gy"), P("gx", "gy", None)),
        check_vma=False,
    )
```

profile of v0, /device:TPU:10, one launch (start us, length us, event | category | flops | bytes accessed | tf_op | source)
XLA Modules:
  0.0 589.0 jit_solution(8751553567018417610)
XLA Ops:
  7.2 0.7 copy.20
  8.8 0.7 fusion.105
  9.7 4.4 fusion.96
  14.4 1.4 fusion.83
  15.8 6.2 %fusion.92 = f32[2304]{0:T(1024)S(1)} fusion(pred[2304]{0:T(1024)(128)(4,1)S(1)} %get-tuple-element.388, pred[2304]{0:T(1024)(128)(4,1)S(1)} %get-tuple-element.387, pred[2304]{0:T(1024)(128)(4,1)S(1)} %get-tuple-element.386, pred[2304]{0:T(1024)(128)(4,1)S(1)} %get-tuple-element.385, pred[2304]{0:T(1024)(128)(4,1)S(1)} %get-tuple-element.384, ...), kind=kLoop, calls=%fused_computation.184 | loop fusion | flops 29952 | bytes 41516 | tf_op jit(solution)/shard_map/convert_element_type | solution.py:25
  22.0 2.0 fusion.82
  24.0 1.0 pad_maximum_fusion
  25.7 84.1 %all-gather.3.cloned.1.call-done = bf16[18432,1,192]{0,2,1:T(8,128)(2,1)} async-done(((bf16[2304,1,192]{0,2,1:T(8,128)(2,1)}), bf16[18432,1,192]{0,2,1:T(8,128)(2,1)}) %all-gather.3.cloned.1.call-update) | async-done | bytes 7077904 | tf_op jit(solution)/shard_map/all_gather | solution.py:106
  109.8 7.0 %copy.26 = bf16[1,24,16,8,1152]{4,3,1,0,2:T(8,128)(2,1)} copy(bf16[1,24,16,8,1152]{4,3,2,1,0:T(8,128)(2,1)} %bitcast.168) | data formatting | bytes 14155776 | tf_op jit(solution)/shard_map/reshape | solution.py:113
  117.0 229.6 %while.32 = (s32[]{:T(128)}, f32[1,576]{1,0:T(1,128)S(1)}, f32[1,576]{1,0:T(1,128)S(1)}, f32[1,576,96]{1,2,0:T(8,128)S(1)}, f32[1,576]{1,0:T(1,128)S(1)}, /*inde...) while((s32[]{:T(128)}, f32[1,576]{1,0:T(1,128)S(1)}, ...), condition=%wide.region_20.21_spmd, body=%wide.region_3.20_spmd.sunk | while | flops 1067440896 | bytes 37980108 | solution.py:140
  117.3 1.1 dynamic-slice_bitcast_fusion.2
  122.6 3.1 conditional.11
  122.8 1.0 fusion.100
  123.8 1.0 fusion.56
  124.8 0.9 fusion.50
  128.2 3.0 conditional.10
  128.3 1.0 fusion.99
  129.3 1.0 fusion.40
  130.3 0.9 fusion.34
  133.8 3.1 conditional.9
  134.0 1.0 fusion.98
  135.0 1.0 fusion.24
  136.0 0.9 fusion.18
  139.4 2.9 conditional.8
  139.5 1.0 fusion.97
  140.5 1.0 fusion.8
  141.4 0.9 fusion.2
  142.4 1.1 dynamic-slice_bitcast_fusion.2
  143.5 0.7 fusion.110
  147.8 3.1 conditional.11
  148.0 1.0 fusion.100
  149.0 1.0 fusion.56
  149.9 0.9 fusion.50
  153.4 2.9 conditional.10
  153.5 1.0 fusion.99
  154.5 1.0 fusion.40
  155.5 0.9 fusion.34
  161.6 1.1 dynamic-slice_bitcast_fusion.2
  174.9 1.1 dynamic-slice_bitcast_fusion.2
  188.1 1.1 dynamic-slice_bitcast_fusion.2
  201.3 1.1 dynamic-slice_bitcast_fusion.2
  214.5 1.1 dynamic-slice_bitcast_fusion.2
  227.7 1.1 dynamic-slice_bitcast_fusion.2
  240.9 1.1 dynamic-slice_bitcast_fusion.2
  254.2 1.1 dynamic-slice_bitcast_fusion.2
  267.4 1.1 dynamic-slice_bitcast_fusion.2
  280.6 1.1 dynamic-slice_bitcast_fusion.2
  293.8 1.1 dynamic-slice_bitcast_fusion.2
  307.0 1.1 dynamic-slice_bitcast_fusion.2
  320.2 1.1 dynamic-slice_bitcast_fusion.2
  333.4 1.1 dynamic-slice_bitcast_fusion.2
  346.8 1.0 concatenate.37
  347.8 0.8 slice.201
  348.6 1.5 collective-permute-start
  350.4 0.7 fusion.104
  351.2 8.8 %fusion.93 = (s32[2319]{0:T(1024)S(1)}, s32[2319]{0:T(1024)S(1)}, s32[2319,1]{0,1:T(1,128)S(1)}) fusion(s32[]{:T(128)} %bitcast.66, s32[]{:T(128)} %bitcast.67, s32[]{:T(128)} %bitcast.68, s32[]{:T(128)} %bitcast.69, s32[]{:T(128)} %bitcast.70, s32[]{:T(128)} %bitcast.72, s32[]{:T(128)} %bitcast.71, s32[]{:T(128)} %bitcast.46, s32[]{:T(128)} %bitcast.45, ...), kind=kLoop, calls=%fused_computation.187 | loop fusion | flops 48699 | bytes 37160 | tf_op jit(solution)/shard_map/gather | solution.py:161
  360.4 6.2 %select_select_fusion.1 = s32[2319]{0:T(1024)S(1)} fusion(pred[2319]{0:T(1024)(128)(4,1)S(1)} %get-tuple-element.378, pred[2319]{0:T(1024)(128)(4,1)S(1)} %get-tuple-element.377, pred[2319]{0:T(1024)(128)(4,1)S(1)} %get-tuple-element.376, pred[2319]{0:T(1024)(128)(4,1)S(1)} %get-tuple-element.375, pred[2319]{0:T(1024)(128)(4,1)S(1)} %get-tuple-element.374, ...), kind=kLoop, calls=%fused_computation.182 | loop fusion | flops 23190 | bytes 41782 | tf_op jit(solution)/shard_map/gather | solution.py:158
  366.6 6.5 %select_select_fusion = s32[2319]{0:T(1024)S(1)} fusion(pred[2319]{0:T(1024)(128)(4,1)S(1)} %get-tuple-element.378, pred[2319]{0:T(1024)(128)(4,1)S(1)} %get-tuple-element.377, pred[2319]{0:T(1024)(128)(4,1)S(1)} %get-tuple-element.376, pred[2319]{0:T(1024)(128)(4,1)S(1)} %get-tuple-element.375, pred[2319]{0:T(1024)(128)(4,1)S(1)} %get-tuple-element.374, ...), kind=kLoop, calls=%fused_computation.181 | loop fusion | flops 23190 | bytes 41782 | tf_op jit(solution)/shard_map/gather | solution.py:161
  373.3 12.7 %gather_fusion = s32[2319]{0:T(1024)S(1)} fusion(s32[1169]{0:T(1024)S(1)} %copy-done, s32[3072]{0:T(1024)S(1)} %pad_clamp_fusion), kind=kCustom, calls=%fused_computation | custom fusion | bytes 27828 | tf_op jit(solution)/shard_map/gather | solution.py:165
  386.4 169.8 %all_gather.11 = bf16[3072,96]{0,1:T(8,128)(2,1)S(1)} all-gather(bf16[384,96]{0,1:T(8,128)(2,1)S(1)} %copy-done.2), channel_id=1, replica_groups=mesh['gx'=8,'gy'=32] {'gx'}, dimensions={0}, use_global_device_ids=true | all-gather | bytes 663552 | tf_op jit(solution)/shard_map/all_gather | solution.py:147
  556.3 1.6 copy.23
  557.9 13.5 %scatter_custom_fusion = bf16[2576,192]{1,0:T(8,128)(2,1)S(1)} fusion(s32[2319]{0:T(1024)S(1)} %broadcast_select_fusion, bf16[2319,192]{1,0:T(8,128)(2,1)} %copy.23, bf16[]{:T(256)} %constant.123.clone.1), kind=kCustom, calls=%fused_computation.81 | custom fusion | bytes 989696
  571.4 2.5 reshape.620
  573.9 8.2 %fusion.64 = bf16[2304,96]{0,1:T(8,128)(2,1)} fusion(bf16[3072,96]{0,1:T(8,128)(2,1)S(1)} %all_gather.11, bf16[2304,3072]{0,1:T(8,128)(2,1)} %all-gather.5.cloned.1.call-done, bf16[2304,96]{0,1:T(8,128)(2,1)S(1)} %copy-done.1), kind=kOutput, calls=%fused_computation.76 | convolution fusion | flops 1359618048 | bytes 15630336 | tf_op jit(solution)/shard_map/dot_general | solution.py:148
  (228 shorter events, 35.3 us)
Async XLA Ops:
  7.2 366.1 %copy-start = (s32[1169]{0:T(1024)S(1)}, s32[1169]{0:T(1024)}, u32[]{:S(2)}) copy-start(s32[1169]{0:T(1024)} %param.16) | copy-start | bytes 14032
  7.2 102.7 %all-gather.3.cloned.1.call-start = ((), (), s32[]{:S(2)}) async-start(), calls=%async_computation | async-start | bytes 7962624 | tf_op jit(solution)/shard_map/all_gather | solution.py:106
  25.0 548.9 %all-gather.5.cloned.1.call-start = ((), (), s32[]{:S(2)}) async-start(), calls=%async_computation.1 | async-start | bytes 14598144 | tf_op jit(solution)/shard_map/all_gather | solution.py:149
  348.6 207.6 %collective-permute-start = (bf16[15,1,192]{0,2,1:T(8,128)(2,1)S(1)}, bf16[15,1,192]{0,2,1:T(8,128)(2,1)S(1)}, u32[]{:S(2)}, u32[]{:S(2)}) collective-permute-start(bf16[15,1,192]{0,2,1:T(8,128)(2,1)S(1)} %slice.201), channel_id=1, source_target_pairs={{32,0},{64,32},{96,64},{128,96},{160,128},{192,160},{224,192},{33,... | collective-permute-start | bytes 17288 | tf_op jit(solution)/shard_map/ppermute | solution.py:15
  373.2 12.9 %copy-start.3 = (s32[2]{0:T(128)S(1)}, s32[2]{0:T(128)}, u32[]{:S(2)}) copy-start(s32[2]{0:T(128)} %constant.132) | copy-start | bytes 28
  373.3 13.0 %copy-start.4 = (s32[2]{0:T(128)S(1)}, s32[2]{0:T(128)}, u32[]{:S(2)}) copy-start(s32[2]{0:T(128)} %constant.135) | copy-start | bytes 28
  373.3 13.1 %copy-start.2 = (bf16[384,96]{0,1:T(8,128)(2,1)S(1)}, bf16[384,96]{0,1:T(8,128)(2,1)}, u32[]{:S(2)}) copy-start(bf16[384,96]{0,1:T(8,128)(2,1)} %param.19) | copy-start | bytes 221188
  556.3 17.7 %copy-start.1 = (bf16[2304,96]{0,1:T(8,128)(2,1)S(1)}, bf16[2304,96]{0,1:T(8,128)(2,1)}, u32[]{:S(2)}) copy-start(bf16[2304,96]{0,1:T(8,128)(2,1)} %param.18) | copy-start | bytes 1327108
Sparse Core Ops, SparseCore 0:
  25.2 84.6 all-gather.2
  347.9 211.4 all-gather.4
where the time goes:
time: 593 us; the launch traced here: 589 us
  blocking collectives  170 us (29%)
  loops' own time  164 us (28%)
  local copies, waits for them, and re-layouts  89.9 us (15%)
  waiting for transfers between devices  84.2 us (14%)
  other arithmetic  45.2 us (8%)
  matrix products  19.9 us (3%)
  between operations  14.4 us (2%)
    all_gather x1, blocking collectives, per_device(): weight_columns = lax.all_gather(out_weight, 'gx', axis=0, tiled=True)  170 us
    another operation x1, loops' own time, per_device(): folded = lax.scan(advance, initial, scanned_input)[0]  163 us
    all_gather x1, waiting for transfers between devices, per_device(): portion = lax.all_gather(key_value, 'gx', axis=0, tiled=True)  84.1 us
    squeeze x16, local copies, waits for them, and re-layouts, per_device(): folded = lax.scan(advance, initial, scanned_input)[0]  16.9 us
    gather x2, other arithmetic, per_device(): logical = page_base[extended_segment] + extended_position // PAGE  15.4 us
    unnamed x11, local copies, waits for them, and re-layouts  13.6 us
    gather x1, local copies, waits for them, and re-layouts, per_device(): page_table[logical] - group_index * pages_held  12.7 us
  transfers between devices with their start and end apart: 3, of which 1 were waited for; matrix products, arithmetic and copies ran while one was open for 9% of the time, Pallas kernels for 0%

commit v1 on v0

--- a/solution.py
+++ b/solution.py
@@ -7,6 +7,13 @@
 
 HD = 96
 PAGE = 16
+
+
+def pack_core_now(out_dim, local):
+    arr_now = jnp.stack(tuple((local for _ in range(lax.axis_size("gx")))), 0)
+    oldest = lax.all_to_all(arr_now, axis_name="gx", split_axis=0, concat_axis=0)
+    left_arr = jnp.concatenate(oldest, axis=out_dim)
+    return left_arr
 
 
 def passed_along(block, axis, distance):
@@ -103,7 +110,7 @@
             for number in range(block_count)
         )
     )
-    portion = lax.all_gather(key_value, "gx", axis=0, tiled=True)
+    portion = pack_core_now(0, key_value)
     key_count = portion.shape[0]
     key_rows = key_count // max(1, key_count // 1152)
     steps_needed = key_count // key_rows

time: 593 us -> 746 us (1.26)
  waiting for transfers between devices: 84.2 us -> 157 us
  blocking collectives: 170 us -> 211 us
  local copies, waits for them, and re-layouts: 89.9 us -> 114 us
  starting transfers between devices: 1.58 us -> 10 us
    all_to_all x0 -> x1, waiting for transfers between devices: none -> 157 us  [pack_core_now(): lax.all_to_all(arr_now, axis_name='gx', split_axis=0, concat_axis=0)]
    all_gather x1 -> x0, waiting for transfers between devices: 84.1 us -> none  [per_device(): portion = lax.all_gather(key_value, 'gx', axis=0, tiled=True)]
    all_gather x1, blocking collectives: 170 us -> 211 us  [per_device(): weight_columns = lax.all_gather(out_weight, 'gx', axis=0, tiled=True)]
    another operation x14 -> x16, local copies, waits for them, and re-layouts: 0.95 us -> 15.4 us  [the longest x1 11.1 us: per_device(): portion.reshape(steps_needed, key_rows, local_heads, 2 * HD)]
    all_to_all x0 -> x1, local copies, waits for them, and re-layouts: none -> 9.82 us  [pack_core_now(): lax.all_to_all(arr_now, axis_name='gx', split_axis=0, concat_axis=0)]
    all_to_all x0 -> x1, starting transfers between devices: none -> 8.47 us  [pack_core_now(): lax.all_to_all(arr_now, axis_name='gx', split_axis=0, concat_axis=0)]
    while x0 -> x1, local copies, waits for them, and re-layouts: none -> 7.59 us  [per_device(): folded = lax.scan(advance, initial, scanned_input)[0]]
  transfers between devices with their start and end apart: 3 -> 3, of which waited for: 1 -> 1; matrix products, arithmetic and copies ran while one was open for 9% -> 7% of each run, Pallas kernels for 0% -> 0%
where the time goes in v1:
time: 746 us; the launch traced here: 741 us
  blocking collectives  211 us (28%)
  loops' own time  164 us (22%)
  waiting for transfers between devices  157 us (21%)
  local copies, waits for them, and re-layouts  114 us (15%)
  other arithmetic  44.7 us (6%)
  matrix products  25.3 us (3%)
  between operations  14.4 us (2%)
  starting transfers between devices  10 us (1%)
    all_gather x1, blocking collectives, per_device(): weight_columns = lax.all_gather(out_weight, 'gx', axis=0, tiled=True)  211 us
    another operation x1, loops' own time, per_device(): folded = lax.scan(advance, initial, scanned_input)[0]  163 us
    all_to_all x1, waiting for transfers between devices, pack_core_now(): lax.all_to_all(arr_now, axis_name='gx', split_axis=0, concat_axis=0)  157 us
    squeeze x16, local copies, waits for them, and re-layouts, per_device(): folded = lax.scan(advance, initial, scanned_input)[0]  16.9 us
    gather x2, other arithmetic, per_device(): logical = page_base[extended_segment] + extended_position // PAGE  15 us
  transfers between devices with their start and end apart: 3, of which 1 were waited for; matrix products, arithmetic and copies ran while one was open for 7% of the time, Pallas kernels for 0%

profile of v1, /device:TPU:10, one launch (start us, length us, event | category | flops | bytes accessed | tf_op | source)
XLA Modules:
  0.0 740.7 jit_solution(9168482104039588510)
XLA Ops:
  7.2 0.7 copy.25
  9.6 4.4 fusion.96
  14.3 1.4 fusion.83
  15.7 6.2 fusion.92
  22.0 2.0 fusion.82
  24.1 3.4 stack.2
  27.5 8.5 %all-to-all-start = ((bf16[8,2304,1,192]{1,3,2,0:T(8,128)(2,1)}), bf16[8,2304,1,192]{1,3,2,0:T(8,128)(2,1)}, u32[]{:S(2)}, u32[]{:S(2)}) async-start(bf16[8,2304,1,192]{1,3,2,0:T(8,128)(2,1)} %stack.2), calls=%async_computation | async-start | bytes 14155776 | tf_op jit(solution)/shard_map/all_to_all | solution.py:14
  36.4 0.8 pad_maximum_fusion.1
  37.3 157.1 %all-to-all-done = bf16[8,2304,1,192]{1,3,2,0:T(8,128)(2,1)} async-done(((bf16[8,2304,1,192]{1,3,2,0:T(8,128)(2,1)}), bf16[8,2304,1,192]{1,3,2,0:T(8,128)(2,1)}, u32[]{:S(2)}, u32[]{:S(2)}) %all-to-all-start) | async-done | bytes 7077920 | tf_op jit(solution)/shard_map/all_to_all | solution.py:14
  194.4 9.8 %copy.26 = bf16[8,2304,1,192]{1,0,3,2:T(8,128)(2,1)} copy(bf16[8,2304,1,192]{1,3,2,0:T(8,128)(2,1)} %all-to-all-done) | data formatting | bytes 14155776 | tf_op jit(solution)/shard_map/all_to_all | solution.py:14
  204.2 11.1 %reshape_reshape.3 = bf16[16,1152,1,192]{1,0,3,2:T(8,128)(2,1)} reshape(bf16[8,2304,1,192]{1,0,3,2:T(8,128)(2,1)} %copy.26) | data formatting | bytes 14155776 | tf_op jit(solution)/shard_map/reshape;reshape | solution.py:120
  215.3 7.6 %copy.27 = bf16[16,1152,1,192]{1,3,2,0:T(8,128)(2,1)} copy(bf16[16,1152,1,192]{1,0,3,2:T(8,128)(2,1)} %reshape_reshape.3) | data formatting | bytes 14155776 | tf_op jit(solution)/shard_map/while | solution.py:147
  223.1 235.0 %while.32 = (s32[]{:T(128)}, f32[1,576]{1,0:T(1,128)S(1)}, f32[1,576]{1,0:T(1,128)S(1)}, f32[1,576,96]{1,2,0:T(8,128)S(1)}, f32[1,576]{1,0:T(1,128)S(1)}, /*inde...) while((s32[]{:T(128)}, f32[1,576]{1,0:T(1,128)S(1)}, ...), condition=%wide.region_20.21_spmd, body=%wide.region_3.20_spmd.sunk | while | flops 1067440896 | bytes 37980108 | solution.py:147
  223.3 1.1 dynamic-slice_bitcast_fusion.2
  228.7 4.0 conditional.11
  228.8 1.9 fusion.101
  230.7 1.0 fusion.56
  231.7 0.9 fusion.50
  235.2 3.9 conditional.10
  235.2 1.9 fusion.100
  237.2 1.0 fusion.40
  238.1 0.9 fusion.34
  241.7 4.0 conditional.9
  241.9 1.9 fusion.99
  243.8 1.0 fusion.24
  244.8 0.9 fusion.18
  248.2 3.9 conditional.8
  248.2 1.9 fusion.98
  250.1 1.0 fusion.8
  251.1 0.9 fusion.2
  252.1 1.1 dynamic-slice_bitcast_fusion.2
  257.5 4.0 conditional.11
  257.7 1.9 fusion.101
  259.6 1.0 fusion.56
  260.5 0.9 fusion.50
  264.0 3.9 conditional.10
  264.1 1.9 fusion.100
  266.0 1.0 fusion.40
  267.0 0.9 fusion.34
  273.2 1.1 dynamic-slice_bitcast_fusion.2
  286.4 1.1 dynamic-slice_bitcast_fusion.2
  299.6 1.1 dynamic-slice_bitcast_fusion.2
  312.8 1.1 dynamic-slice_bitcast_fusion.2
  326.0 1.1 dynamic-slice_bitcast_fusion.2
  339.2 1.1 dynamic-slice_bitcast_fusion.2
  352.4 1.1 dynamic-slice_bitcast_fusion.2
  365.7 1.1 dynamic-slice_bitcast_fusion.2
  378.9 1.1 dynamic-slice_bitcast_fusion.2
  392.1 1.1 dynamic-slice_bitcast_fusion.2
  405.3 1.1 dynamic-slice_bitcast_fusion.2
  418.5 1.1 dynamic-slice_bitcast_fusion.2
  431.7 1.1 dynamic-slice_bitcast_fusion.2
  445.0 1.1 dynamic-slice_bitcast_fusion.2
  458.3 1.0 concatenate.40
  459.3 1.5 collective-permute-start
  462.0 8.8 %fusion.93 = (s32[2319]{0:T(1024)S(1)}, s32[2319]{0:T(1024)S(1)}, s32[2319,1]{0,1:T(1,128)S(1)}) fusion(s32[]{:T(128)} %bitcast.67, s32[]{:T(128)} %bitcast.68, s32[]{:T(128)} %bitcast.69, s32[]{:T(128)} %bitcast.70, s32[]{:T(128)} %bitcast.71, s32[]{:T(128)} %bitcast.73, s32[]{:T(128)} %bitcast.72, s32[]{:T(128)} %bitcast.46, s32[]{:T(128)} %bitcast.45, ...), kind=kLoop, calls=%fused_computation.186 | loop fusion | flops 48699 | bytes 37160 | tf_op jit(solution)/shard_map/gather | solution.py:168
  471.0 6.2 select_select_fusion.1
  477.3 6.2 select_select_fusion
  483.7 12.7 %gather_fusion = s32[2319]{0:T(1024)S(1)} fusion(s32[1169]{0:T(1024)S(1)} %copy-done, s32[3072]{0:T(1024)S(1)} %pad_clamp_fusion), kind=kCustom, calls=%fused_computation | custom fusion | bytes 27828 | tf_op jit(solution)/shard_map/gather | solution.py:172
  496.8 211.1 %all_gather.7 = bf16[3072,96]{0,1:T(8,128)(2,1)S(1)} all-gather(bf16[384,96]{0,1:T(8,128)(2,1)S(1)} %copy-done.2), channel_id=1, replica_groups=mesh['gx'=8,'gy'=32] {'gx'}, dimensions={0}, use_global_device_ids=true | all-gather | bytes 663552 | tf_op jit(solution)/shard_map/all_gather | solution.py:154
  708.0 1.6 copy.29
  709.6 13.5 %scatter_custom_fusion = bf16[2576,192]{1,0:T(8,128)(2,1)S(1)} fusion(s32[2319]{0:T(1024)S(1)} %broadcast_select_fusion, bf16[2319,192]{1,0:T(8,128)(2,1)} %copy.29, bf16[]{:T(256)} %constant.123.clone.1), kind=kCustom, calls=%fused_computation.80 | custom fusion | bytes 989696
  723.1 2.5 reshape.619
  725.6 8.2 %fusion.64 = bf16[2304,96]{0,1:T(8,128)(2,1)} fusion(bf16[3072,96]{0,1:T(8,128)(2,1)S(1)} %all_gather.7, bf16[2304,3072]{0,1:T(8,128)(2,1)} %all-gather.2.cloned.1.call-done, bf16[2304,96]{0,1:T(8,128)(2,1)S(1)} %copy-done.1), kind=kOutput, calls=%fused_computation.75 | convolution fusion | flops 1359618048 | bytes 15630336 | tf_op jit(solution)/shard_map/dot_general | solution.py:155
  (230 shorter events, 37.3 us)
Async XLA Ops:
  7.2 476.5 %copy-start = (s32[1169]{0:T(1024)S(1)}, s32[1169]{0:T(1024)}, u32[]{:S(2)}) copy-start(s32[1169]{0:T(1024)} %param.16) | copy-start | bytes 14032
  27.5 166.9 %all-to-all-start = ((bf16[8,2304,1,192]{1,3,2,0:T(8,128)(2,1)}), bf16[8,2304,1,192]{1,3,2,0:T(8,128)(2,1)}, u32[]{:S(2)}, u32[]{:S(2)}) async-start(bf16[8,2304,1,192]{1,3,2,0:T(8,128)(2,1)} %stack.2), calls=%async_computation | async-start | bytes 14155776 | tf_op jit(solution)/shard_map/all_to_all | solution.py:14
  36.0 689.6 %all-gather.2.cloned.1.call-start = ((), (), s32[]{:S(2)}) async-start(), calls=%async_computation.1 | async-start | bytes 14598144 | tf_op jit(solution)/shard_map/all_gather | solution.py:156
  459.3 248.6 %collective-permute-start = (bf16[15,1,192]{0,2,1:T(8,128)(2,1)S(1)}, bf16[15,1,192]{0,2,1:T(8,128)(2,1)S(1)}, u32[]{:S(2)}, u32[]{:S(2)}) collective-permute-start(bf16[15,1,192]{0,2,1:T(8,128)(2,1)S(1)} %slice.201), channel_id=1, source_target_pairs={{32,0},{64,32},{96,64},{128,96},{160,128},{192,160},{224,192},{33,... | collective-permute-start | bytes 17288 | tf_op jit(solution)/shard_map/ppermute | solution.py:22
  483.6 12.9 %copy-start.3 = (s32[2]{0:T(128)S(1)}, s32[2]{0:T(128)}, u32[]{:S(2)}) copy-start(s32[2]{0:T(128)} %constant.132) | copy-start | bytes 28
  483.7 13.0 %copy-start.4 = (s32[2]{0:T(128)S(1)}, s32[2]{0:T(128)}, u32[]{:S(2)}) copy-start(s32[2]{0:T(128)} %constant.135) | copy-start | bytes 28
  483.7 13.1 %copy-start.2 = (bf16[384,96]{0,1:T(8,128)(2,1)S(1)}, bf16[384,96]{0,1:T(8,128)(2,1)}, u32[]{:S(2)}) copy-start(bf16[384,96]{0,1:T(8,128)(2,1)} %param.19) | copy-start | bytes 221188
  708.0 17.6 %copy-start.1 = (bf16[2304,96]{0,1:T(8,128)(2,1)S(1)}, bf16[2304,96]{0,1:T(8,128)(2,1)}, u32[]{:S(2)}) copy-start(bf16[2304,96]{0,1:T(8,128)(2,1)} %param.18) | copy-start | bytes 1327108
Sparse Core Ops, SparseCore 0:
  459.4 253.1 all-gather.1
